TPU v7x, 128 devices: a whole 4x4x4 slice. The times are simulated.
128 devices in a mesh: row: 8 (over x, core), col: 16 (over y, z).
Axes of the slice: x: 4, y: 4, z: 4, core: 2. Of those that a mesh axis runs over, the one named last changes fastest.
Arguments:
- front_matrix: float32 [16384, 16384], P('row', 'col'), may hold values from -2.5 to 202.5, as said below
- child_schur: float32 [2, 8192, 8192], P(None, 'row', 'col'), may hold values from -1.25 to 1.25
- child_index: int32 [2, 128], replicated, may hold values from 0 to 255, as said below
- child_valid: int32 [2, 128], replicated, may hold values 0 or 1
Outputs:
- trailing: float32 [16384, 16384], P('row', 'col')
- panel_factor: float32 [16384, 512], P('row')
Inputs may be any that keep to these rules, and one draw needn't show every extreme that they name: `front_matrix`: off the logical diagonal the entries lie in -2.5 to 2.5, on it in 97.5 to 202.5. `child_index`: each child's 128 entries are distinct front blocks. Among the child blocks a that share a mod 8, exactly 2 land in front blocks of each value mod 8; among the child blocks b that share b mod 16, at most 1 land in front blocks of any one value mod 16, and some value takes exactly 1.
All inputs are finite; a program needn't handle non-finite values.
Results may differ from a plain program's by a relative error of at most 0.00005.
Values sent between devices are 32-bit elements; how exact they have to be, the bound alone decides.
No kernel may reach another device: no remote copies, remote signals or barrier semaphores. Data moves between devices by JAX's collectives and lax.ppermute only.
A program may use at most 256 MiB of HBM per device.

v0:
```python
import jax
import jax.numpy as jnp
from jax import lax
from jax.sharding import PartitionSpec as P

CHILD = 8192
PANEL = 512
BLK = 64
exact_mode = lax.Precision.HIGHEST


def take_slabs(source, indices):
    return jnp.take(source, indices, axis=0)


def on_device(front_matrix, child_schur, child_index, child_valid):
    row_count = lax.axis_size("row")
    col_count = lax.axis_size("col")
    row_place = lax.axis_index("row")
    col_place = lax.axis_index("col")
    local_rows, local_cols = front_matrix.shape
    row_blocks = local_rows // BLK
    col_blocks = local_cols // BLK
    child_blocks = CHILD // BLK
    child_rowblk = child_schur.shape[1] // BLK
    child_colblk = child_schur.shape[2] // BLK
    per_owner = child_blocks // (row_count * row_count)
    col_multi = max(1, child_blocks // (col_count * col_count))
    row_slots = row_count * per_owner
    col_slots = col_count * col_multi
    validity = child_valid.astype(jnp.float32)
    all_blocks = jnp.arange(child_blocks)
    owner_row = child_index % row_count
    owner_col = child_index % col_count
    sender_row = all_blocks % row_count
    sender_col = all_blocks % col_count
    before = all_blocks[None, :] < all_blocks[:, None]
    earlier_row = (sender_row[:, None] == sender_row[None, :]) & before
    earlier_col = (sender_col[:, None] == sender_col[None, :]) & before
    row_rank = jnp.sum(
        (earlier_row[None] & (owner_row[:, :, None] == owner_row[:, None, :])).astype(jnp.int32),
        axis=2,
    )
    col_rank = jnp.sum(
        (earlier_col[None] & (owner_col[:, :, None] == owner_col[:, None, :])).astype(jnp.int32),
        axis=2,
    )
    row_key = owner_row * per_owner + row_rank
    col_key = owner_col * col_multi + col_rank
    local_arow = row_place + row_count * jnp.arange(child_rowblk)
    mine_rowkey = jnp.take(row_key, local_arow, axis=1)
    row_hit_send = mine_rowkey[:, :, None] == jnp.arange(row_slots)[None, None, :]
    src_row = jnp.sum(
        row_hit_send.astype(jnp.int32) * jnp.arange(child_rowblk)[None, :, None], axis=1
    )
    local_bcol = col_place + col_count * jnp.arange(child_colblk)
    mine_colkey = jnp.take(col_key, local_bcol, axis=1)
    col_hit_send = mine_colkey[:, :, None] == jnp.arange(col_slots)[None, None, :]
    src_col = jnp.sum(
        col_hit_send.astype(jnp.int32) * jnp.arange(child_colblk)[None, :, None], axis=1
    )
    has_col = jnp.sum(col_hit_send.astype(jnp.float32), axis=1)
    blocks = child_schur.reshape(2, child_rowblk, BLK, child_colblk * BLK)
    outgoing = jax.vmap(take_slabs)(blocks, src_row)
    outgoing = outgoing.reshape(2, row_slots * BLK, child_colblk * BLK)
    section_one = lax.all_to_all(outgoing, "row", split_axis=1, concat_axis=1, tiled=True)
    flipped = jnp.swapaxes(section_one, 1, 2).reshape(2, child_colblk, BLK, row_slots * BLK)
    onward = jax.vmap(take_slabs)(flipped, src_col) * has_col[:, :, None, None]
    onward = onward.reshape(2, col_slots * BLK, row_slots * BLK)
    section_two = lax.all_to_all(onward, "col", split_axis=1, concat_axis=1, tiled=True)
    arrived = section_two.reshape(2, col_slots, BLK, row_slots * BLK)
    front_rowblk = row_place + row_count * jnp.arange(row_blocks)
    match_rows = (child_index[:, None, :] == front_rowblk[None, :, None]).astype(jnp.int32)
    row_slot_of = sender_row[None, :] * per_owner + row_rank
    row_source = jnp.sum(match_rows * row_slot_of[:, None, :], axis=2)
    row_weight = jnp.sum(match_rows.astype(jnp.float32) * validity[:, None, :], axis=2)
    front_colblk = col_place + col_count * jnp.arange(col_blocks)
    match_cols = (child_index[:, None, :] == front_colblk[None, :, None]).astype(jnp.int32)
    col_slot_of = sender_col[None, :] * col_multi + col_rank
    col_source = jnp.sum(match_cols * col_slot_of[:, None, :], axis=2)
    col_weight = jnp.sum(match_cols.astype(jnp.float32) * validity[:, None, :], axis=2)
    by_col = jax.vmap(take_slabs)(arrived, col_source) * col_weight[:, :, None, None]
    by_col = by_col.reshape(2, local_cols, row_slots * BLK)
    unflipped = jnp.swapaxes(by_col, 1, 2).reshape(2, row_slots, BLK, local_cols)
    placed = jax.vmap(take_slabs)(unflipped, row_source) * row_weight[:, :, None, None]
    placed = placed.reshape(2, local_rows, local_cols)
    extended = front_matrix + placed[0] + placed[1]
    panel_width = PANEL // BLK
    spread = col_count // panel_width
    lead = extended[:, :BLK]
    lifted = lax.ppermute(
        lead,
        "col",
        [(c, c + panel_width * s) for s in range(1, spread) for c in range(panel_width)],
    )
    mine = jnp.where(col_place < panel_width, lead, lifted)
    part_rows = local_rows // spread
    part = lax.dynamic_slice_in_dim(mine, col_place // panel_width * part_rows, part_rows, axis=0)
    gathered = lax.all_gather(part, "col", axis=0, tiled=False)
    gathered = gathered.reshape(spread, panel_width, part_rows, BLK)
    panel_cols = gathered.transpose(0, 2, 1, 3).reshape(local_rows, PANEL)
    corner = lax.all_gather(panel_cols[: PANEL // row_count], "row", axis=0, tiled=True)
    lower_factor = jnp.linalg.cholesky(corner)
    solved = jax.scipy.linalg.solve_triangular(lower_factor, panel_cols.T, lower=True).T
    logical_blk = jnp.arange(row_blocks) * row_count + row_place
    factor_blocks = lower_factor.reshape(panel_width, BLK, PANEL)
    picked = jnp.take(factor_blocks, jnp.minimum(logical_blk, panel_width - 1), axis=0)
    in_panel = (logical_blk < panel_width)[:, None, None]
    panel_factor = jnp.where(in_panel, picked, solved.reshape(row_blocks, BLK, PANEL)).reshape(
        local_rows, PANEL
    )
    ratio = col_count // row_count
    arranged = panel_factor.reshape(col_blocks, ratio, BLK, PANEL)
    chosen = lax.dynamic_index_in_dim(arranged, col_place // row_count, axis=1, keepdims=False)
    chosen = chosen.reshape(col_blocks * BLK, PANEL)
    pairs = []
    for r0 in range(row_count):
        for c1 in range(col_count):
            dest_row = c1 % row_count
            dest_col = r0 + row_count * (c1 // row_count)
            pairs.append((r0 * col_count + c1, dest_row * col_count + dest_col))
    across = lax.ppermute(chosen, ("row", "col"), pairs)
    update = jnp.einsum("rp,cp->rc", panel_factor, across, precision=exact_mode)
    logical_row = jnp.arange(local_rows) // BLK * row_count + row_place
    logical_col = jnp.arange(local_cols) // BLK * col_count + col_place
    retained = (logical_row >= panel_width)[:, None] & (logical_col >= panel_width)[None, :]
    trailing = jnp.where(retained, extended - update, jnp.zeros_like(update))
    return (trailing, panel_factor)


def solution(mesh):
    in_specs = (P("row", "col"), P(None, "row", "col"), P(), P())
    out_specs = (P("row", "col"), P("row", None))
    return jax.shard_map(
        on_device, mesh=mesh, in_specs=in_specs, out_specs=out_specs, check_vma=False
    )
```

profile of v0, /device:TPU:7, one launch (start us, length us, event | category | flops | bytes accessed | tf_op | source)
XLA Modules:
  0.0 768.0 jit_solution(1678104543497816341)
XLA Ops:
  10.7 5.0 gather_fusion.3
  15.7 2.5 bitcast_select_fusion.2
  18.2 5.2 copy.126
  23.4 5.1 all-to-all-start
  29.0 46.6 %all-to-all-done = f32[2,1024,512]{2,0,1:T(2,128)} async-done(((f32[2,1024,512]{2,0,1:T(2,128)}), f32[2,1024,512]{2,0,1:T(2,128)}, u32[]{:S(2)}, u32[]{:S(2)}) %all-to-all-start) | async-done | bytes 4194336 | tf_op jit(solution)/shard_map/all_to_all | solution.py:66
  75.6 7.2 copy.127
  82.8 6.7 gather_fusion.4
  89.5 3.9 fusion.2
  93.4 12.9 %copy.128 = f32[2,1024,1024]{2,0,1:T(2,128)} copy(f32[2,1024,1024]{2,1,0:T(8,128)S(1)} %fusion.2) | data formatting | bytes 16777216 | tf_op jit(solution)/shard_map/mul | solution.py:68
  106.3 8.1 %all-to-all-start.1 = ((f32[2,1024,1024]{2,0,1:T(2,128)}), f32[2,1024,1024]{2,0,1:T(2,128)}, u32[]{:S(2)}, u32[]{:S(2)}) async-start(f32[2,1024,1024]{2,0,1:T(2,128)} %copy.128), calls=%async_computation.1 | async-start | bytes 16777216 | tf_op jit(solution)/shard_map/all_to_all | solution.py:70
  115.9 140.9 %all-to-all-done.1 = f32[2,1024,1024]{2,0,1:T(2,128)} async-done(((f32[2,1024,1024]{2,0,1:T(2,128)}), f32[2,1024,1024]{2,0,1:T(2,128)}, u32[]{:S(2)}, u32[]{:S(2)}) %all-to-all-start.1) | async-done | bytes 8388640 | tf_op jit(solution)/shard_map/all_to_all | solution.py:70
  256.8 9.5 %copy.129 = f32[2,1024,1024]{2,1,0:T(8,128)} copy(f32[2,1024,1024]{2,0,1:T(2,128)} %all-to-all-done.1) | data formatting | bytes 16777216 | tf_op jit(solution)/shard_map/all_to_all | solution.py:70
  266.3 7.7 %gather_fusion.5 = f32[32,64,1024]{2,1,0:T(8,128)} fusion(f32[2,16,64,1024]{3,2,1,0:T(8,128)} %bitcast.129, s32[32]{0:T(128)S(1)} %reshape.535), kind=kCustom, calls=%fused_computation.5 | custom fusion | bytes 16777472 | tf_op jit(solution)/shard_map/vmap(jit(_take))/gather | solution.py:13
  274.0 6.0 fusion.1
  280.0 8.7 %copy.130 = f32[2,1024,1024]{2,1,0:T(8,128)} copy(f32[2,1024,1024]{1,2,0:T(8,128)} %fusion.1) | data formatting | bytes 16777216 | tf_op jit(solution)/shard_map/transpose | solution.py:84
  288.7 12.5 %gather_fusion.6 = f32[64,64,1024]{2,1,0:T(8,128)} fusion(f32[2,16,64,1024]{3,2,1,0:T(8,128)} %bitcast.124, s32[64]{0:T(128)S(1)} %reshape.541), kind=kCustom, calls=%fused_computation.6 | custom fusion | bytes 33554944 | tf_op jit(solution)/shard_map/vmap(jit(_take))/gather | solution.py:13
  301.2 7.3 select_multiply_fusion
  308.5 6.7 fusion.77
  315.2 9.7 %bitcast_add_fusion = f32[2048,1024]{1,0:T(8,128)S(1)} fusion(f32[1,32,64,1024]{3,2,1,0:T(8,128)} %get-tuple-element.35, f32[2048,1024]{1,0:T(8,128)} %param.4, f32[1,32,64,1024]{3,2,1,0:T(8,128)} %get-tuple-element.34), kind=kLoop, calls=%fused_computation.10 | loop fusion | flops 4194304 | bytes 33554432 | tf_op jit(solution)/shard_map/add | solution.py:87
  325.0 3.4 copy-done
  328.8 1.3 collective-permute-start
  330.2 8.5 %collective-permute-done = f32[2048,64]{0,1:T(8,128)S(1)} collective-permute-done((f32[2048,64]{0,1:T(8,128)S(1)}, f32[2048,64]{0,1:T(8,128)S(1)}, u32[]{:S(2)}, u32[]{:S(2)}) %collective-permute-start) | collective-permute-done | bytes 524320 | tf_op jit(solution)/shard_map/ppermute | solution.py:91
  338.9 0.9 dynamic-slice_select_fusion.2
  339.9 84.5 %all-gather.6.cloned.1.call-done = f32[16384,64]{1,0:T(8,128)} async-done(((f32[1024,64]{1,0:T(8,128)}), f32[16384,64]{1,0:T(8,128)}) %all-gather.6.cloned.1.call-update) | async-done | bytes 4194320 | tf_op jit(solution)/shard_map/all_gather | solution.py:99
  424.4 9.0 %copy.133 = f32[2,8,1024,64]{2,0,3,1:T(2,128)} copy(f32[2,8,1024,64]{3,2,1,0:T(8,128)} %bitcast.141) | data formatting | bytes 8388608 | tf_op jit(solution)/shard_map/reshape | solution.py:100
  433.4 4.1 copy.142
  437.6 2.0 copy-done.1
  439.6 0.8 copy.134
  440.8 21.5 %all-gather.4.cloned.1.call-done = f32[512,512]{1,0:T(8,128)} async-done(((f32[64,512]{1,0:T(8,128)}), f32[512,512]{1,0:T(8,128)}) %all-gather.4.cloned.1.call-update) | async-done | bytes 1048592 | tf_op jit(solution)/shard_map/all_gather | solution.py:102
  462.3 1.6 copy.135
  463.9 1.4 fusion.17
  465.3 11.7 %cholesky.104 = f32[128,128]{1,0:T(8,128)S(1)} custom-call(f32[128,128]{1,0:T(8,128)S(1)} %cholesky.266), custom_call_target="Cholesky" | custom-call | tf_op jit(solution)/shard_map/jit(cholesky)/cholesky | solution.py:103
  477.2 9.8 %custom-call.31 = f32[1,128,128]{1,2,0:T(8,128)S(1)} custom-call(f32[1,128,128]{2,1,0:T(8,128)S(1)} %get-tuple-element.45), custom_call_target="InvertDiagBlocksLowerTriangular" | custom-call | tf_op jit(solution)/shard_map/jit(cholesky)/cholesky | solution.py:103
  487.7 11.9 %cholesky.217 = f32[128,128]{1,0:T(8,128)S(1)} custom-call(f32[128,128]{1,0:T(8,128)S(1)} %cholesky.270), custom_call_target="Cholesky" | custom-call | tf_op jit(solution)/shard_map/jit(cholesky)/cholesky | solution.py:103
  500.2 0.7 compare_reduce_fusion.3
  500.9 9.8 %custom-call.32 = f32[1,128,128]{1,2,0:T(8,128)S(1)} custom-call(f32[1,128,128]{2,1,0:T(8,128)S(1)} %get-tuple-element.42), custom_call_target="InvertDiagBlocksLowerTriangular" | custom-call | tf_op jit(solution)/shard_map/jit(cholesky)/cholesky | solution.py:103
  511.4 11.7 %cholesky.238 = f32[128,128]{1,0:T(8,128)S(1)} custom-call(f32[128,128]{1,0:T(8,128)S(1)} %cholesky.275), custom_call_target="Cholesky" | custom-call | tf_op jit(solution)/shard_map/jit(cholesky)/cholesky | solution.py:103
  523.8 9.8 %custom-call.33 = f32[1,128,128]{1,2,0:T(8,128)S(1)} custom-call(f32[1,128,128]{2,1,0:T(8,128)S(1)} %get-tuple-element.39), custom_call_target="InvertDiagBlocksLowerTriangular" | custom-call | tf_op jit(solution)/shard_map/jit(cholesky)/cholesky | solution.py:103
  534.2 11.9 %cholesky.255 = f32[128,128]{1,0:T(8,128)S(1)} custom-call(f32[128,128]{1,0:T(8,128)S(1)} %convolution_subtract_fusion.4), custom_call_target="Cholesky" | custom-call | tf_op jit(solution)/shard_map/jit(cholesky)/cholesky | solution.py:103
  546.2 0.7 compare_reduce_fusion
  549.7 10.5 %while.1 = (s32[]{:T(128)}, f32[512,512]{1,0:T(8,128)S(1)}, s32[4,2]{0,1:T(2,128)S(1)}, f32[4,128,128]{2,1,0:T(8,128)}, s32[]{:T(128)}) while((s32[]{:T(128)}, f32[512,512]{1,0:T(8,128)S(1)}, s32[4,2]{0,1:T(2,128)S(1)}, f32[4,128,128]{2,1,0:T(8,128)}, s32[]{:T(128)}) %tuple.44), condition=%wide.while_cond, body=%wide.while_body.sunk | while | flops 2 | bytes 132705 | solution.py:104
  550.4 2.0 bitcast_dynamic-update-slice_fusion.2
  553.0 2.0 bitcast_dynamic-update-slice_fusion.2
  555.6 2.0 bitcast_dynamic-update-slice_fusion.2
  558.3 2.0 bitcast_dynamic-update-slice_fusion.2
  560.2 40.2 %custom-call.34 = f32[4,128,128]{1,2,0:T(8,128)S(1)} custom-call(f32[4,128,128]{2,1,0:T(8,128)} %get-tuple-element.9), custom_call_target="InvertDiagBlocksLowerTriangular" | custom-call | tf_op jit(solution)/shard_map/jit(_solve_triangular)/triangular_solve | solution.py:104
  600.4 2.4 fusion.15
  602.8 2.2 convolution_subtract_fusion.1
  605.1 1.1 fusion.30
  606.2 2.2 convolution_subtract_fusion
  608.3 1.1 fusion.28
  609.4 3.2 fusion.9
  612.6 1.0 fusion.27
  613.7 1.1 copy-done.5
  614.7 2.4 maximum_bitcast_fusion
  617.1 5.3 copy.139
  622.5 2.8 gather_fusion.2
  625.3 4.2 dynamic-slice_select_fusion
  629.5 7.2 collective-permute-start.1
  637.1 5.7 copy.136
  642.8 5.4 select_select_fusion
  648.2 5.3 copy.140
  653.5 75.5 %collective-permute-done.1 = f32[1024,512]{1,0:T(8,128)} collective-permute-done((f32[1024,512]{1,0:T(8,128)}, f32[1024,512]{1,0:T(8,128)}, u32[]{:S(2)}, u32[]{:S(2)}) %collective-permute-start.1) | collective-permute-done | bytes 2097184 | tf_op jit(solution)/shard_map/ppermute | solution.py:122
  729.1 31.7 %subtract_select_fusion = f32[2048,1024]{1,0:T(8,128)} fusion(f32[2048,1024]{1,0:T(8,128)} %copy-done, pred[1024]{0:T(1024)(128)(4,1)S(1)} %fusion.54, pred[2048]{0:T(1024)(128)(4,1)S(1)} %fusion.48, f32[2048,512]{0,1:T(8,128)} %select_select_fusion, f32[1024,512]{1,0:T(8,128)} %collective-permute-done.1), kind=kOutput, calls=%fused_computation.17 | convolution fusion | flops 12891193344 | bytes 23071744 | tf_op jit(solution)/shard_map/rp,cp->rc/dot_general | solution.py:123
  (121 shorter events, 13.3 us)
Async XLA Ops:
  23.4 52.2 %all-to-all-start = ((f32[2,1024,512]{2,0,1:T(2,128)}), f32[2,1024,512]{2,0,1:T(2,128)}, u32[]{:S(2)}, u32[]{:S(2)}) async-start(f32[2,1024,512]{2,0,1:T(2,128)} %copy.126), calls=%async_computation | async-start | bytes 8388608 | tf_op jit(solution)/shard_map/all_to_all | solution.py:66
  106.3 8.3 %copy-start.7 = (s32[2,128]{1,0:T(2,128)S(1)}, s32[2,128]{1,0:T(2,128)}, u32[]{:S(2)}) copy-start(s32[2,128]{1,0:T(2,128)} %param.6) | copy-start | bytes 3076
  106.3 8.8 %copy-start.8 = (s32[2,128]{1,0:T(2,128)S(1)}, s32[2,128]{1,0:T(2,128)}, u32[]{:S(2)}) copy-start(s32[2,128]{1,0:T(2,128)} %param.7) | copy-start | bytes 3076
  106.3 150.5 %all-to-all-start.1 = ((f32[2,1024,1024]{2,0,1:T(2,128)}), f32[2,1024,1024]{2,0,1:T(2,128)}, u32[]{:S(2)}, u32[]{:S(2)}) async-start(f32[2,1024,1024]{2,0,1:T(2,128)} %copy.128), calls=%async_computation.1 | async-start | bytes 16777216 | tf_op jit(solution)/shard_map/all_to_all | solution.py:70
  114.4 310.0 %all-gather.6.cloned.1.call-start = ((), (), s32[]{:S(2)}) async-start(), calls=%async_computation.3 | async-start | bytes 8912896 | tf_op jit(solution)/shard_map/all_gather | solution.py:99
  325.0 3.4 copy-start
  328.8 9.9 %collective-permute-start = (f32[2048,64]{0,1:T(8,128)S(1)}, f32[2048,64]{0,1:T(8,128)S(1)}, u32[]{:S(2)}, u32[]{:S(2)}) collective-permute-start(f32[2048,64]{0,1:T(8,128)S(1)} %copy.131), channel_id=1, source_target_pairs={{0,8},{1,9},{2,10},{3,11},{4,12},{5,13},{6,14},{7,15},{16,24},{17,... | collective-permute-start | bytes 1572872 | tf_op jit(solution)/shard_map/ppermute | solution.py:91
  339.8 122.5 %all-gather.4.cloned.1.call-start = ((), (), s32[]{:S(2)}) async-start(), calls=%async_computation.2 | async-start | bytes 1179648 | tf_op jit(solution)/shard_map/all_gather | solution.py:102
  437.6 2.0 copy-start.1
  560.2 42.6 %copy-start.6 = (f32[512,512]{1,0:T(8,128)}, f32[512,512]{1,0:T(8,128)S(1)}, u32[]{:S(2)}) copy-start(f32[512,512]{1,0:T(8,128)S(1)} %get-tuple-element.112) | copy-start | bytes 3145732
  600.4 5.7 copy-start.2
  609.4 4.2 copy-start.3
  613.7 1.1 copy-start.5
  629.5 99.5 %collective-permute-start.1 = (f32[1024,512]{1,0:T(8,128)}, f32[1024,512]{1,0:T(8,128)}, u32[]{:S(2)}, u32[]{:S(2)}) collective-permute-start(f32[1024,512]{1,0:T(8,128)} %bitcast.40), channel_id=1, source_target_pairs={{0,0},{1,16},{2,32},{3,48},{4,64},{5,80},{6,96},{7,112},{8,8},{9,2... | collective-permute-start | bytes 6291464 | tf_op jit(solution)/shard_map/ppermute | solution.py:122
  637.1 5.7 copy-start.4
Sparse Core Ops, SparseCore 0:
  339.9 84.4 all-gather.5
  440.5 21.7 all-gather.3
where the time goes:
time: 777 us; the launch traced here: 768 us
  waiting for transfers between devices  378 us (49%)
  other arithmetic  166 us (21%)
  local copies, waits for them, and re-layouts  138 us (18%)
  matrix products  46.7 us (6%)
  starting transfers between devices  22 us (3%)
  between operations  17.6 us (2%)
    all_to_all x1, waiting for transfers between devices, on_device(): lax.all_to_all(onward, 'col', split_axis=1, concat_axis=1, tiled=True)  141 us
    all_gather x1, waiting for transfers between devices, on_device(): gathered = lax.all_gather(part, 'col', axis=0, tiled=False)  84.5 us
    another operation x15, other arithmetic, on_device(): lower_factor = jnp.linalg.cholesky(corner)  79.5 us
    ppermute x1, waiting for transfers between devices, on_device(): across = lax.ppermute(chosen, ('row', 'col'), pairs)  75.5 us
    all_to_all x1, waiting for transfers between devices, on_device(): lax.all_to_all(outgoing, 'row', split_axis=1, concat_axis=1, tiled=True)  46.6 us
    another operation x3, other arithmetic, on_device(): jax.scipy.linalg.solve_triangular(lower_factor, panel_cols.T, lower=True)  40.4 us
    gather x8, local copies, waits for them, and re-layouts, take_slabs(): return jnp.take(source, indices, axis=0)  32.2 us
    dot_general x1, matrix products, on_device(): update = jnp.einsum('rp,cp->rc', panel_factor, across, precision=exact_mode)  31.7 us
  transfers between devices with their start and end apart: 6, of which 6 were waited for; matrix products, arithmetic and copies ran while one was open for 2% of the time, Pallas kernels for 0%

commit v1 on v0

--- a/solution.py
+++ b/solution.py
@@ -63,7 +63,14 @@
     blocks = child_schur.reshape(2, child_rowblk, BLK, child_colblk * BLK)
     outgoing = jax.vmap(take_slabs)(blocks, src_row)
     outgoing = outgoing.reshape(2, row_slots * BLK, child_colblk * BLK)
-    section_one = lax.all_to_all(outgoing, "row", split_axis=1, concat_axis=1, tiled=True)
+
+    def derive_clusters_now(which_axis, z):
+        return jnp.concatenate(
+            lax.all_to_all(jnp.stack(jnp.split(z, lax.axis_size(which_axis), 1)), which_axis, 0, 0),
+            1,
+        )
+
+    section_one = derive_clusters_now("row", z=outgoing)
     flipped = jnp.swapaxes(section_one, 1, 2).reshape(2, child_colblk, BLK, row_slots * BLK)
     onward = jax.vmap(take_slabs)(flipped, src_col) * has_col[:, :, None, None]
     onward = onward.reshape(2, col_slots * BLK, row_slots * BLK)

time: 777 us -> 779 us (level)
    unnamed x21 -> x28, local copies, waits for them, and re-layouts: 16.2 us -> 22 us
where the time goes in v1:
time: 779 us; the launch traced here: 772 us
  waiting for transfers between devices  378 us (49%)
  other arithmetic  166 us (21%)
  local copies, waits for them, and re-layouts  142 us (18%)
  matrix products  46.7 us (6%)
  starting transfers between devices  22 us (3%)
  between operations  17.6 us (2%)
    all_to_all x1, waiting for transfers between devices, on_device(): lax.all_to_all(onward, 'col', split_axis=1, concat_axis=1, tiled=True)  141 us
    all_gather x1, waiting for transfers between devices, on_device(): gathered = lax.all_gather(part, 'col', axis=0, tiled=False)  84.5 us
    another operation x15, other arithmetic, on_device(): lower_factor = jnp.linalg.cholesky(corner)  79.5 us
    ppermute x1, waiting for transfers between devices, on_device(): across = lax.ppermute(chosen, ('row', 'col'), pairs)  75.5 us
    all_to_all x1, waiting for transfers between devices, derive_clusters_now(): lax.all_to_all(jnp.stack(jnp.split(z, lax.axis_size(which_axis), 1)), whi...  46.6 us
    another operation x3, other arithmetic, on_device(): jax.scipy.linalg.solve_triangular(lower_factor, panel_cols.T, lower=True)  40.4 us
    gather x8, local copies, waits for them, and re-layouts, take_slabs(): return jnp.take(source, indices, axis=0)  32.2 us
    dot_general x1, matrix products, on_device(): update = jnp.einsum('rp,cp->rc', panel_factor, across, precision=exact_mode)  31.7 us
  transfers between devices with their start and end apart: 6, of which 6 were waited for; matrix products, arithmetic and copies ran while one was open for 2% of the time, Pallas kernels for 0%

profile of v1, /device:TPU:7, one launch (start us, length us, event | category | flops | bytes accessed | tf_op | source)
XLA Modules:
  0.0 772.4 jit_solution(8623027801980188069)
XLA Ops:
  10.7 5.0 gather_fusion.3
  15.7 2.5 bitcast_select_fusion.2
  18.2 0.8 fusion.26
  19.0 0.8 fusion.25
  19.8 0.8 fusion.24
  24.8 5.1 all-to-all-start
  30.4 46.6 %all-to-all-done = f32[8,2,128,512]{3,2,1,0:T(8,128)} async-done(((f32[8,2,128,512]{3,2,1,0:T(8,128)}), f32[8,2,128,512]{3,2,1,0:T(8,128)}, u32[]{:S(2)}, u32[]{:S(2)}) %all-to-all-start) | async-done | bytes 4194336 | tf_op jit(solution)/shard_map/all_to_all | solution.py:69
  77.0 4.8 copy.141
  81.8 5.4 copy.142
  87.2 6.7 gather_fusion.4
  93.9 3.9 fusion.2
  97.8 12.9 %copy.143 = f32[2,1024,1024]{2,0,1:T(2,128)} copy(f32[2,1024,1024]{2,1,0:T(8,128)S(1)} %fusion.2) | data formatting | bytes 16777216 | tf_op jit(solution)/shard_map/mul | solution.py:75
  110.7 8.1 %all-to-all-start.1 = ((f32[2,1024,1024]{2,0,1:T(2,128)}), f32[2,1024,1024]{2,0,1:T(2,128)}, u32[]{:S(2)}, u32[]{:S(2)}) async-start(f32[2,1024,1024]{2,0,1:T(2,128)} %copy.143), calls=%async_computation.1 | async-start | bytes 16777216 | tf_op jit(solution)/shard_map/all_to_all | solution.py:77
  120.3 140.9 %all-to-all-done.1 = f32[2,1024,1024]{2,0,1:T(2,128)} async-done(((f32[2,1024,1024]{2,0,1:T(2,128)}), f32[2,1024,1024]{2,0,1:T(2,128)}, u32[]{:S(2)}, u32[]{:S(2)}) %all-to-all-start.1) | async-done | bytes 8388640 | tf_op jit(solution)/shard_map/all_to_all | solution.py:77
  261.2 9.5 %copy.144 = f32[2,1024,1024]{2,1,0:T(8,128)} copy(f32[2,1024,1024]{2,0,1:T(2,128)} %all-to-all-done.1) | data formatting | bytes 16777216 | tf_op jit(solution)/shard_map/all_to_all | solution.py:77
  270.7 7.7 gather_fusion.5
  278.4 6.0 fusion.1
  284.4 8.7 %copy.145 = f32[2,1024,1024]{2,1,0:T(8,128)} copy(f32[2,1024,1024]{1,2,0:T(8,128)} %fusion.1) | data formatting | bytes 16777216 | tf_op jit(solution)/shard_map/transpose | solution.py:91
  293.1 12.5 %gather_fusion.6 = f32[64,64,1024]{2,1,0:T(8,128)} fusion(f32[2,16,64,1024]{3,2,1,0:T(8,128)} %bitcast.159, s32[64]{0:T(128)S(1)} %reshape.549), kind=kCustom, calls=%fused_computation.6 | custom fusion | bytes 33554944 | tf_op jit(solution)/shard_map/vmap(jit(_take))/gather | solution.py:13
  305.6 7.3 select_multiply_fusion
  312.9 6.7 fusion.85
  319.6 9.7 %bitcast_add_fusion = f32[2048,1024]{1,0:T(8,128)S(1)} fusion(f32[1,32,64,1024]{3,2,1,0:T(8,128)} %get-tuple-element.35, f32[2048,1024]{1,0:T(8,128)} %param.4, f32[1,32,64,1024]{3,2,1,0:T(8,128)} %get-tuple-element.34), kind=kLoop, calls=%fused_computation.10 | loop fusion | flops 4194304 | bytes 33554432 | tf_op jit(solution)/shard_map/add | solution.py:94
  329.4 3.4 copy-done
  333.2 1.3 collective-permute-start
  334.6 8.5 %collective-permute-done = f32[2048,64]{0,1:T(8,128)S(1)} collective-permute-done((f32[2048,64]{0,1:T(8,128)S(1)}, f32[2048,64]{0,1:T(8,128)S(1)}, u32[]{:S(2)}, u32[]{:S(2)}) %collective-permute-start) | collective-permute-done | bytes 524320 | tf_op jit(solution)/shard_map/ppermute | solution.py:98
  343.4 0.9 dynamic-slice_select_fusion.2
  344.3 84.5 %all-gather.6.cloned.1.call-done = f32[16384,64]{1,0:T(8,128)} async-done(((f32[1024,64]{1,0:T(8,128)}), f32[16384,64]{1,0:T(8,128)}) %all-gather.6.cloned.1.call-update) | async-done | bytes 4194320 | tf_op jit(solution)/shard_map/all_gather | solution.py:106
  428.8 9.0 %copy.148 = f32[2,8,1024,64]{2,0,3,1:T(2,128)} copy(f32[2,8,1024,64]{3,2,1,0:T(8,128)} %bitcast.177) | data formatting | bytes 8388608 | tf_op jit(solution)/shard_map/reshape | solution.py:107
  437.8 4.1 copy.157
  442.0 2.0 copy-done.1
  445.2 21.5 %all-gather.4.cloned.1.call-done = f32[512,512]{1,0:T(8,128)} async-done(((f32[64,512]{1,0:T(8,128)}), f32[512,512]{1,0:T(8,128)}) %all-gather.4.cloned.1.call-update) | async-done | bytes 1048592 | tf_op jit(solution)/shard_map/all_gather | solution.py:109
  466.7 1.6 copy.150
  468.3 1.4 fusion.17
  469.7 11.7 %cholesky.104 = f32[128,128]{1,0:T(8,128)S(1)} custom-call(f32[128,128]{1,0:T(8,128)S(1)} %cholesky.266), custom_call_target="Cholesky" | custom-call | tf_op jit(solution)/shard_map/jit(cholesky)/cholesky | solution.py:110
  481.6 9.8 %custom-call.31 = f32[1,128,128]{1,2,0:T(8,128)S(1)} custom-call(f32[1,128,128]{2,1,0:T(8,128)S(1)} %get-tuple-element.45), custom_call_target="InvertDiagBlocksLowerTriangular" | custom-call | tf_op jit(solution)/shard_map/jit(cholesky)/cholesky | solution.py:110
  492.1 11.9 %cholesky.217 = f32[128,128]{1,0:T(8,128)S(1)} custom-call(f32[128,128]{1,0:T(8,128)S(1)} %cholesky.270), custom_call_target="Cholesky" | custom-call | tf_op jit(solution)/shard_map/jit(cholesky)/cholesky | solution.py:110
  505.4 9.8 %custom-call.32 = f32[1,128,128]{1,2,0:T(8,128)S(1)} custom-call(f32[1,128,128]{2,1,0:T(8,128)S(1)} %get-tuple-element.42), custom_call_target="InvertDiagBlocksLowerTriangular" | custom-call | tf_op jit(solution)/shard_map/jit(cholesky)/cholesky | solution.py:110
  515.8 11.7 %cholesky.238 = f32[128,128]{1,0:T(8,128)S(1)} custom-call(f32[128,128]{1,0:T(8,128)S(1)} %cholesky.275), custom_call_target="Cholesky" | custom-call | tf_op jit(solution)/shard_map/jit(cholesky)/cholesky | solution.py:110
  528.2 9.8 %custom-call.33 = f32[1,128,128]{1,2,0:T(8,128)S(1)} custom-call(f32[1,128,128]{2,1,0:T(8,128)S(1)} %get-tuple-element.39), custom_call_target="InvertDiagBlocksLowerTriangular" | custom-call | tf_op jit(solution)/shard_map/jit(cholesky)/cholesky | solution.py:110
  538.7 11.9 %cholesky.255 = f32[128,128]{1,0:T(8,128)S(1)} custom-call(f32[128,128]{1,0:T(8,128)S(1)} %convolution_subtract_fusion.4), custom_call_target="Cholesky" | custom-call | tf_op jit(solution)/shard_map/jit(cholesky)/cholesky | solution.py:110
  554.1 10.5 %while.1 = (s32[]{:T(128)}, f32[512,512]{1,0:T(8,128)S(1)}, s32[4,2]{0,1:T(2,128)S(1)}, f32[4,128,128]{2,1,0:T(8,128)}, s32[]{:T(128)}) while((s32[]{:T(128)}, f32[512,512]{1,0:T(8,128)S(1)}, s32[4,2]{0,1:T(2,128)S(1)}, f32[4,128,128]{2,1,0:T(8,128)}, s32[]{:T(128)}) %tuple.45), condition=%wide.while_cond, body=%wide.while_body.sunk | while | flops 2 | bytes 132705 | solution.py:111
  554.8 2.0 bitcast_dynamic-update-slice_fusion.2
  557.4 2.0 bitcast_dynamic-update-slice_fusion.2
  560.1 2.0 bitcast_dynamic-update-slice_fusion.2
  562.7 2.0 bitcast_dynamic-update-slice_fusion.2
  564.6 40.2 %custom-call.34 = f32[4,128,128]{1,2,0:T(8,128)S(1)} custom-call(f32[4,128,128]{2,1,0:T(8,128)} %get-tuple-element.9), custom_call_target="InvertDiagBlocksLowerTriangular" | custom-call | tf_op jit(solution)/shard_map/jit(_solve_triangular)/triangular_solve | solution.py:111
  604.8 2.4 fusion.15
  607.3 2.2 convolution_subtract_fusion.1
  609.5 1.1 fusion.38
  610.6 2.2 convolution_subtract_fusion
  612.8 1.1 fusion.36
  613.8 3.2 fusion.9
  617.0 1.0 fusion.35
  618.1 1.1 copy-done.5
  619.1 2.4 maximum_bitcast_fusion
  621.5 5.3 copy.154
  626.9 2.8 gather_fusion.2
  629.7 4.2 dynamic-slice_select_fusion
  633.9 7.2 collective-permute-start.1
  641.6 5.7 copy.151
  647.2 5.4 select_select_fusion
  652.6 5.3 copy.155
  657.9 75.5 %collective-permute-done.1 = f32[1024,512]{1,0:T(8,128)} collective-permute-done((f32[1024,512]{1,0:T(8,128)}, f32[1024,512]{1,0:T(8,128)}, u32[]{:S(2)}, u32[]{:S(2)}) %collective-permute-start.1) | collective-permute-done | bytes 2097184 | tf_op jit(solution)/shard_map/ppermute | solution.py:129
  733.4 31.7 %subtract_select_fusion = f32[2048,1024]{1,0:T(8,128)} fusion(f32[2048,1024]{1,0:T(8,128)} %copy-done, pred[1024]{0:T(1024)(128)(4,1)S(1)} %fusion.62, pred[2048]{0:T(1024)(128)(4,1)S(1)} %fusion.56, f32[2048,512]{0,1:T(8,128)} %select_select_fusion, f32[1024,512]{1,0:T(8,128)} %collective-permute-done.1), kind=kOutput, calls=%fused_computation.17 | convolution fusion | flops 12891193344 | bytes 23071744 | tf_op jit(solution)/shard_map/rp,cp->rc/dot_general | solution.py:130
  (128 shorter events, 19.6 us)
Async XLA Ops:
  24.8 52.2 %all-to-all-start = ((f32[8,2,128,512]{3,2,1,0:T(8,128)}), f32[8,2,128,512]{3,2,1,0:T(8,128)}, u32[]{:S(2)}, u32[]{:S(2)}) async-start(f32[8,2,128,512]{3,2,1,0:T(8,128)} %fusion.19), calls=%async_computation | async-start | bytes 8388608 | tf_op jit(solution)/shard_map/all_to_all | solution.py:69
  110.7 8.3 %copy-start.7 = (s32[2,128]{1,0:T(2,128)S(1)}, s32[2,128]{1,0:T(2,128)}, u32[]{:S(2)}) copy-start(s32[2,128]{1,0:T(2,128)} %param.6) | copy-start | bytes 3076
  110.7 8.8 %copy-start.8 = (s32[2,128]{1,0:T(2,128)S(1)}, s32[2,128]{1,0:T(2,128)}, u32[]{:S(2)}) copy-start(s32[2,128]{1,0:T(2,128)} %param.7) | copy-start | bytes 3076
  110.7 150.5 %all-to-all-start.1 = ((f32[2,1024,1024]{2,0,1:T(2,128)}), f32[2,1024,1024]{2,0,1:T(2,128)}, u32[]{:S(2)}, u32[]{:S(2)}) async-start(f32[2,1024,1024]{2,0,1:T(2,128)} %copy.143), calls=%async_computation.1 | async-start | bytes 16777216 | tf_op jit(solution)/shard_map/all_to_all | solution.py:77
  118.8 310.0 %all-gather.6.cloned.1.call-start = ((), (), s32[]{:S(2)}) async-start(), calls=%async_computation.3 | async-start | bytes 8912896 | tf_op jit(solution)/shard_map/all_gather | solution.py:106
  329.4 3.4 copy-start
  333.2 9.9 %collective-permute-start = (f32[2048,64]{0,1:T(8,128)S(1)}, f32[2048,64]{0,1:T(8,128)S(1)}, u32[]{:S(2)}, u32[]{:S(2)}) collective-permute-start(f32[2048,64]{0,1:T(8,128)S(1)} %copy.146), channel_id=1, source_target_pairs={{0,8},{1,9},{2,10},{3,11},{4,12},{5,13},{6,14},{7,15},{16,24},{17,... | collective-permute-start | bytes 1572872 | tf_op jit(solution)/shard_map/ppermute | solution.py:98
  344.2 122.5 %all-gather.4.cloned.1.call-start = ((), (), s32[]{:S(2)}) async-start(), calls=%async_computation.2 | async-start | bytes 1179648 | tf_op jit(solution)/shard_map/all_gather | solution.py:109
  442.0 2.0 copy-start.1
  564.6 42.6 %copy-start.6 = (f32[512,512]{1,0:T(8,128)}, f32[512,512]{1,0:T(8,128)S(1)}, u32[]{:S(2)}) copy-start(f32[512,512]{1,0:T(8,128)S(1)} %get-tuple-element.112) | copy-start | bytes 3145732
  604.8 5.7 copy-start.2
  613.8 4.2 copy-start.3
  618.1 1.1 copy-start.5
  633.9 99.5 %collective-permute-start.1 = (f32[1024,512]{1,0:T(8,128)}, f32[1024,512]{1,0:T(8,128)}, u32[]{:S(2)}, u32[]{:S(2)}) collective-permute-start(f32[1024,512]{1,0:T(8,128)} %bitcast.50), channel_id=1, source_target_pairs={{0,0},{1,16},{2,32},{3,48},{4,64},{5,80},{6,96},{7,112},{8,8},{9,2... | collective-permute-start | bytes 6291464 | tf_op jit(solution)/shard_map/ppermute | solution.py:129
  641.5 5.7 copy-start.4
Sparse Core Ops, SparseCore 0:
  344.4 84.4 all-gather.5
  444.9 21.7 all-gather.3
